TPU v7x, 32 devices: a whole 2x2x4 slice. The times are simulated.
32 devices in a mesh: ens: 2 (over x), tile: 8 (over z, y), comp: 2 (over core).
Axes of the slice: x: 2, y: 2, z: 4, core: 2. Of those that a mesh axis runs over, the one named last changes fastest.
Arguments:
- increment: bfloat16 [64, 128, 256], P(('ens', 'tile'), None, 'comp'), parts along dimension 0, may hold values from -6 to 6
- land_sea: int32 [32, 128], P('tile'), may hold values 0 or 1
- kernel_x: float32 [41, 256], P(None, 'comp'), may hold values from -1 to 1
- kernel_y: float32 [41, 256], P(None, 'comp'), may hold values from -1 to 1
- balance: bfloat16 [8, 256, 256], P('tile', 'comp'), may hold values from -0.375 to 0.375
Outputs:
- filtered: bfloat16 [64, 128, 256], P('ens', 'tile', 'comp'), parts along dimension 0
There are 2 independent parts, one for each index of `ens`. A program takes and returns all parts, laid end to end along the dimension named above; an argument that names none is the same for every part. Nothing has to cross between parts.
All inputs are finite; a program needn't handle non-finite values. No bound on the sum of `land_sea` on one device may be relied on, other than what follows from the above.
Results may differ from a plain program's by a relative error of at most 0.0057.
Values may be sent and summed in bfloat16 or wider, within the bound.
No kernel may reach another device: no remote copies, remote signals or barrier semaphores. Data moves between devices by JAX's collectives and lax.ppermute only.
A program may use at most 64 MiB of HBM per device.

v0:
```python
import jax
import jax.numpy as jnp
from jax import lax
from jax.sharding import PartitionSpec as P


def zonal_filter(values, kernel):
    taps = kernel.shape[0]
    half_taps = (taps - 1) // 2
    total = jnp.zeros(values.shape, jnp.float32)
    for offset in range(taps):
        total = total + kernel[offset] * jnp.roll(values, half_taps - offset, axis=1)
    return total


def meridional_filter(values, kernel):
    taps = kernel.shape[0]
    half_taps = (taps - 1) // 2
    rows_all = values.shape[0]
    padded = jnp.pad(values, ((half_taps, half_taps), (0, 0), (0, 0)))
    total = jnp.zeros(values.shape, jnp.float32)
    for offset in range(taps):
        total = total + kernel[offset] * padded[offset : offset + rows_all]
    return total


def to_columns(row_bands):
    return lax.all_to_all(row_bands, "tile", split_axis=1, concat_axis=0, tiled=True)


def per_device(increment, land_sea, kernel_x, kernel_y, balance):
    sea = land_sea.astype(jnp.bfloat16)[:, :, None]
    masked = increment * sea
    zonal = (zonal_filter(masked, kernel_x) * sea.astype(jnp.float32)).astype(jnp.bfloat16)
    own_block = balance[0]
    mixed_rows = jnp.dot(
        lax.all_gather(zonal, "comp", axis=2, tiled=True),
        own_block.T,
        preferred_element_type=jnp.float32,
    )
    mixed = to_columns(mixed_rows.astype(jnp.bfloat16))
    return meridional_filter(mixed, kernel_y).astype(jnp.bfloat16)


def solution(mesh):
    return jax.shard_map(
        per_device,
        mesh=mesh,
        in_specs=(
            P(("ens", "tile"), None, "comp"),
            P("tile", None),
            P(None, "comp"),
            P(None, "comp"),
            P("tile", "comp", None),
        ),
        out_specs=P("ens", "tile", "comp"),
        check_vma=False,
    )
```

profile of v0, /device:TPU:0, one launch (start us, length us, event | category | flops | bytes accessed | tf_op | source)
XLA Modules:
  0.0 26.5 jit_solution(1189334224262708944)
XLA Ops:
  0.0 0.0 copy-start
  0.0 0.7 %fusion.1 = (f32[4,128]{1,0:T(4,128)S(1)}, bf16[4,128]{1,0:T(4,128)(2,1)S(1)}) fusion(s32[4,128]{1,0:T(4,128)} %param.6), kind=kLoop, calls=%fused_computation.127 | loop fusion | flops 1024 | bytes 5120 | tf_op jit(solution)/shard_map/convert_element_type | solution.py:34
  0.7 1.0 %broadcast_multiply_fusion = bf16[4,128,128]{2,1,0:T(8,128)(2,1)S(1)} fusion(bf16[4,128,128]{2,1,0:T(8,128)(2,1)} %param.5, bf16[4,128]{1,0:T(4,128)(2,1)S(1)} %get-tuple-element.6), kind=kLoop, calls=%fused_computation.44 | loop fusion | flops 65536 | bytes 263168 | tf_op jit(solution)/shard_map/mul | solution.py:33
  3.0 0.0 copy-start.2
  3.1 0.7 %copy-done.2 = f32[41,128]{1,0:T(8,128)S(1)} copy-done((f32[41,128]{1,0:T(8,128)S(1)}, f32[41,128]{1,0:T(8,128)}, u32[]{:S(2)}) %copy-start.2) | copy-done | bytes 21016
  3.8 0.0 copy-start.1
  3.8 0.9 %copy-done.1 = bf16[4,128,128]{2,1,0:T(8,128)(2,1)S(1)} copy-done((bf16[4,128,128]{2,1,0:T(8,128)(2,1)S(1)}, bf16[4,128,128]{2,1,0:T(8,128)(2,1)}, u32[]{:S(2)}) %copy-start.1) | copy-done | bytes 131096
  4.7 2.4 %multiply_convert_fusion = bf16[4,128,128]{2,1,0:T(8,128)(2,1)S(1)} fusion(bf16[4,108,128]{2,1,0:T(8,128)(2,1)S(1)} %get-tuple-element.8, bf16[4,20,128]{2,1,0:T(8,128)(2,1)S(1)} %get-tuple-element.10, bf16[4,109,128]{2,1,0:T(8,128)(2,1)S(1)} %get-tuple-element.12, bf16[4,19,128]{2,1,0:T(8,128)(2,1)S(1)} %get-tuple-element.14, ...), kind=kLoop, calls=%fused_computation.42 | loop fusion | flops 16187392 | bytes 5529088 | tf_op jit(solution)/shard_map/convert_element_type | solution.py:34
  7.1 2.1 %all_gather.3 = bf16[4,128,256]{2,1,0:T(8,128)(2,1)S(1)} all-gather(bf16[4,128,128]{2,1,0:T(8,128)(2,1)S(1)} %multiply_convert_fusion), channel_id=1, replica_groups=mesh['ens'=2,'tile'=8,'comp'=2] {'comp'}, dimensions={2}, use_global_device_ids=true | all-gather | bytes 393216 | tf_op jit(solution)/shard_map/all_gather | solution.py:37
  9.2 0.0 copy-done
  9.2 0.2 convolution_convert_fusion
  9.4 0.8 %copy.7 = bf16[4,128,128]{2,0,1:T(4,128)(2,1)} copy(bf16[4,128,128]{2,1,0:T(8,128)(2,1)S(1)} %convolution_convert_fusion) | data formatting | bytes 262144 | tf_op jit(solution)/shard_map/convert_element_type | solution.py:41
  10.2 0.0 copy-start.3
  10.2 7.3 %all-to-all-start = ((bf16[4,128,128]{2,0,1:T(4,128)(2,1)}), bf16[4,128,128]{2,0,1:T(4,128)(2,1)S(1)}, u32[]{:S(2)}, u32[]{:S(2)}) async-start(bf16[4,128,128]{2,0,1:T(4,128)(2,1)} %copy.7), calls=%async_computation | async-start | bytes 262144 | tf_op jit(solution)/shard_map/all_to_all | solution.py:28
  17.5 0.0 copy-done.3
  17.6 7.3 %all-to-all-done = bf16[4,128,128]{2,0,1:T(4,128)(2,1)S(1)} async-done(((bf16[4,128,128]{2,0,1:T(4,128)(2,1)}), bf16[4,128,128]{2,0,1:T(4,128)(2,1)S(1)}, u32[]{:S(2)}, u32[]{:S(2)}) %all-to-all-start) | async-done | bytes 131104 | tf_op jit(solution)/shard_map/all_to_all | solution.py:28
  24.9 1.6 %add_convert_fusion = bf16[32,16,128]{2,1,0:T(8,128)(2,1)} fusion(bf16[32,16,128]{2,1,0:T(8,128)(2,1)S(1)} %bitcast.174, f32[128]{0:T(128)S(1)} %get-tuple-element.126, f32[128]{0:T(128)S(1)} %get-tuple-element.127, f32[128]{0:T(128)S(1)} %get-tuple-element.88, f32[128]{0:T(128)S(1)} %get-tuple-element.89, f32[128]{0:T(128)S(1)} %get-tuple-element.90, ...), kind=kLoop, calls=%fused_computation.41 | loop fusion | flops 8060928 | bytes 283136 | tf_op jit(solution)/shard_map/convert_element_type | solution.py:42
  (47 shorter events, 1.1 us)
Async XLA Ops:
  0.0 9.2 %copy-start = (bf16[1,128,256]{2,1,0:T(8,128)(2,1)S(1)}, bf16[1,128,256]{2,1,0:T(8,128)(2,1)}, u32[]{:S(2)}) copy-start(bf16[1,128,256]{2,1,0:T(8,128)(2,1)} %param.9) | copy-start | bytes 196612
  3.0 0.7 %copy-start.2 = (f32[41,128]{1,0:T(8,128)S(1)}, f32[41,128]{1,0:T(8,128)}, u32[]{:S(2)}) copy-start(f32[41,128]{1,0:T(8,128)} %param.7) | copy-start | bytes 62980
  3.8 0.9 %copy-start.1 = (bf16[4,128,128]{2,1,0:T(8,128)(2,1)S(1)}, bf16[4,128,128]{2,1,0:T(8,128)(2,1)}, u32[]{:S(2)}) copy-start(bf16[4,128,128]{2,1,0:T(8,128)(2,1)} %param.5) | copy-start | bytes 393220
  10.2 7.3 %copy-start.3 = (f32[41,128]{1,0:T(8,128)S(1)}, f32[41,128]{1,0:T(8,128)}, u32[]{:S(2)}) copy-start(f32[41,128]{1,0:T(8,128)} %param.8) | copy-start | bytes 62980
  10.2 14.7 %all-to-all-start = ((bf16[4,128,128]{2,0,1:T(4,128)(2,1)}), bf16[4,128,128]{2,0,1:T(4,128)(2,1)S(1)}, u32[]{:S(2)}, u32[]{:S(2)}) async-start(bf16[4,128,128]{2,0,1:T(4,128)(2,1)} %copy.7), calls=%async_computation | async-start | bytes 262144 | tf_op jit(solution)/shard_map/all_to_all | solution.py:28
where the time goes:
time: 26.9 us; the launch traced here: 26.5 us
  starting transfers between devices  7.32 us (27%)
  waiting for transfers between devices  7.28 us (27%)
  other arithmetic  5.79 us (22%)
  local copies, waits for them, and re-layouts  3.41 us (13%)
  blocking collectives  2.09 us (8%)
  between operations  0.41 us (2%)
    all_to_all x1, starting transfers between devices, to_columns(): lax.all_to_all(row_bands, 'tile', split_axis=1, concat_axis=0, tiled=True)  7.32 us
    all_to_all x1, waiting for transfers between devices, to_columns(): lax.all_to_all(row_bands, 'tile', split_axis=1, concat_axis=0, tiled=True)  7.28 us
    convert_element_type x1, other arithmetic, per_device(): (zonal_filter(masked, kernel_x) * sea.astype(jnp.float32)).astype(jnp.bfl...  2.42 us
    all_gather x1, blocking collectives, per_device(): lax.all_gather(zonal, 'comp', axis=2, tiled=True)  2.09 us
    convert_element_type x1, other arithmetic, per_device(): return meridional_filter(mixed, kernel_y).astype(jnp.bfloat16)  1.63 us
    unnamed x8, local copies, waits for them, and re-layouts  1.54 us
    mul x1, other arithmetic, per_device(): masked = increment * sea  1.03 us
    slice x40, local copies, waits for them, and re-layouts, zonal_filter(): jnp.roll(values, half_taps - offset, axis=1)  1.03 us
  transfers between devices with their start and end apart: 1, of which 1 were waited for; matrix products, arithmetic and copies ran while one was open for 0% of the time, Pallas kernels for 0%

commit v1 on v0

--- a/solution.py
+++ b/solution.py
@@ -25,7 +25,12 @@
 
 
 def to_columns(row_bands):
-    return lax.all_to_all(row_bands, "tile", split_axis=1, concat_axis=0, tiled=True)
+    return jnp.concatenate(
+        lax.all_to_all(
+            jnp.stack(jnp.split(row_bands, lax.axis_size("tile"), axis=1)), "tile", 0, 0
+        ),
+        axis=0,
+    )
 
 
 def per_device(increment, land_sea, kernel_x, kernel_y, balance):

time: 26.9 us -> 30.9 us (1.15)
  local copies, waits for them, and re-layouts: 3.41 us -> 7.49 us
    unnamed x8 -> x15, local copies, waits for them, and re-layouts: 1.54 us -> 5.8 us
    convert_element_type x1 -> x0, local copies, waits for them, and re-layouts: 0.76 us -> none  [per_device(): mixed = to_columns(mixed_rows.astype(jnp.bfloat16))]
    another operation x0 -> x1, local copies, waits for them, and re-layouts: none -> 0.61 us  [to_columns(): jnp.stack(jnp.split(row_bands, lax.axis_size('tile'), axis=1))]
where the time goes in v1:
time: 30.9 us; the launch traced here: 30.5 us
  local copies, waits for them, and re-layouts  7.49 us (24%)
  starting transfers between devices  7.32 us (24%)
  waiting for transfers between devices  7.28 us (24%)
  other arithmetic  5.71 us (18%)
  blocking collectives  2.09 us (7%)
  between operations  0.41 us (1%)
    all_to_all x1, starting transfers between devices, to_columns(): lax.all_to_all(jnp.stack(jnp.split(row_bands, lax.axis_size('tile'), axis...  7.32 us
    all_to_all x1, waiting for transfers between devices, to_columns(): lax.all_to_all(jnp.stack(jnp.split(row_bands, lax.axis_size('tile'), axis...  7.28 us
    unnamed x15, local copies, waits for them, and re-layouts  5.8 us
    convert_element_type x1, other arithmetic, per_device(): (zonal_filter(masked, kernel_x) * sea.astype(jnp.float32)).astype(jnp.bfl...  2.42 us
    all_gather x1, blocking collectives, per_device(): lax.all_gather(zonal, 'comp', axis=2, tiled=True)  2.09 us
    convert_element_type x1, other arithmetic, per_device(): return meridional_filter(mixed, kernel_y).astype(jnp.bfloat16)  1.54 us
    mul x1, other arithmetic, per_device(): masked = increment * sea  1.03 us
    slice x40, local copies, waits for them, and re-layouts, zonal_filter(): jnp.roll(values, half_taps - offset, axis=1)  1.03 us
  transfers between devices with their start and end apart: 1, of which 1 were waited for; matrix products, arithmetic and copies ran while one was open for 0% of the time, Pallas kernels for 0%

profile of v1, /device:TPU:0, one launch (start us, length us, event | category | flops | bytes accessed | tf_op | source)
XLA Modules:
  0.0 30.5 jit_solution(12755372123217632514)
XLA Ops:
  0.0 0.0 copy-start
  0.0 0.7 %fusion.1 = (f32[4,128]{1,0:T(4,128)S(1)}, bf16[4,128]{1,0:T(4,128)(2,1)S(1)}) fusion(s32[4,128]{1,0:T(4,128)} %param.6), kind=kLoop, calls=%fused_computation.143 | loop fusion | flops 1024 | bytes 5120 | tf_op jit(solution)/shard_map/convert_element_type | solution.py:39
  0.7 1.0 %broadcast_multiply_fusion = bf16[4,128,128]{2,1,0:T(8,128)(2,1)S(1)} fusion(bf16[4,128,128]{2,1,0:T(8,128)(2,1)} %param.5, bf16[4,128]{1,0:T(4,128)(2,1)S(1)} %get-tuple-element.6), kind=kLoop, calls=%fused_computation.44 | loop fusion | flops 65536 | bytes 263168 | tf_op jit(solution)/shard_map/mul | solution.py:38
  3.0 0.0 copy-start.2
  3.1 0.7 %copy-done.2 = f32[41,128]{1,0:T(8,128)S(1)} copy-done((f32[41,128]{1,0:T(8,128)S(1)}, f32[41,128]{1,0:T(8,128)}, u32[]{:S(2)}) %copy-start.2) | copy-done | bytes 21016
  3.8 0.0 copy-start.1
  3.8 0.9 %copy-done.1 = bf16[4,128,128]{2,1,0:T(8,128)(2,1)S(1)} copy-done((bf16[4,128,128]{2,1,0:T(8,128)(2,1)S(1)}, bf16[4,128,128]{2,1,0:T(8,128)(2,1)}, u32[]{:S(2)}) %copy-start.1) | copy-done | bytes 131096
  4.7 2.4 %multiply_convert_fusion = bf16[4,128,128]{2,1,0:T(8,128)(2,1)S(1)} fusion(bf16[4,108,128]{2,1,0:T(8,128)(2,1)S(1)} %get-tuple-element.8, bf16[4,20,128]{2,1,0:T(8,128)(2,1)S(1)} %get-tuple-element.10, bf16[4,109,128]{2,1,0:T(8,128)(2,1)S(1)} %get-tuple-element.12, bf16[4,19,128]{2,1,0:T(8,128)(2,1)S(1)} %get-tuple-element.14, ...), kind=kLoop, calls=%fused_computation.42 | loop fusion | flops 16187392 | bytes 5529088 | tf_op jit(solution)/shard_map/convert_element_type | solution.py:39
  7.1 2.1 %all_gather.3 = bf16[4,128,256]{2,1,0:T(8,128)(2,1)S(1)} all-gather(bf16[4,128,128]{2,1,0:T(8,128)(2,1)S(1)} %multiply_convert_fusion), channel_id=1, replica_groups=mesh['ens'=2,'tile'=8,'comp'=2] {'comp'}, dimensions={2}, use_global_device_ids=true | all-gather | bytes 393216 | tf_op jit(solution)/shard_map/all_gather | solution.py:42
  9.2 0.0 copy-done
  9.2 0.2 convolution_convert_fusion
  9.4 0.6 %constant_dynamic-update-slice_fusion.7 = bf16[8,4,16,128]{3,2,1,0:T(8,128)(2,1)} fusion(bf16[4,128,128]{2,1,0:T(8,128)(2,1)S(1)} %convolution_convert_fusion), kind=kLoop, calls=%fused_computation.52 | loop fusion | bytes 32768
  10.0 0.6 %constant_dynamic-update-slice_fusion.6 = bf16[8,4,16,128]{3,2,1,0:T(8,128)(2,1)} fusion(bf16[8,4,16,128]{3,2,1,0:T(8,128)(2,1)} %constant_dynamic-update-slice_fusion.7, bf16[4,128,128]{2,1,0:T(8,128)(2,1)S(1)} %convolution_convert_fusion), kind=kLoop, calls=%fused_computation.51 | loop fusion | bytes 32768
  10.7 0.6 %constant_dynamic-update-slice_fusion.5 = bf16[8,4,16,128]{3,2,1,0:T(8,128)(2,1)} fusion(bf16[8,4,16,128]{3,2,1,0:T(8,128)(2,1)} %constant_dynamic-update-slice_fusion.6, bf16[4,128,128]{2,1,0:T(8,128)(2,1)S(1)} %convolution_convert_fusion), kind=kLoop, calls=%fused_computation.50 | loop fusion | bytes 32768
  11.3 0.6 %constant_dynamic-update-slice_fusion.4 = bf16[8,4,16,128]{3,2,1,0:T(8,128)(2,1)} fusion(bf16[8,4,16,128]{3,2,1,0:T(8,128)(2,1)} %constant_dynamic-update-slice_fusion.5, bf16[4,128,128]{2,1,0:T(8,128)(2,1)S(1)} %convolution_convert_fusion), kind=kLoop, calls=%fused_computation.49 | loop fusion | bytes 32768
  11.9 0.6 %constant_dynamic-update-slice_fusion.3 = bf16[8,4,16,128]{3,2,1,0:T(8,128)(2,1)} fusion(bf16[8,4,16,128]{3,2,1,0:T(8,128)(2,1)} %constant_dynamic-update-slice_fusion.4, bf16[4,128,128]{2,1,0:T(8,128)(2,1)S(1)} %convolution_convert_fusion), kind=kLoop, calls=%fused_computation.48 | loop fusion | bytes 32768
  12.5 0.6 %constant_dynamic-update-slice_fusion.2 = bf16[8,4,16,128]{3,2,1,0:T(8,128)(2,1)} fusion(bf16[8,4,16,128]{3,2,1,0:T(8,128)(2,1)} %constant_dynamic-update-slice_fusion.3, bf16[4,128,128]{2,1,0:T(8,128)(2,1)S(1)} %convolution_convert_fusion), kind=kLoop, calls=%fused_computation.47 | loop fusion | bytes 32768
  13.1 0.6 %constant_dynamic-update-slice_fusion.1 = bf16[8,4,16,128]{3,2,1,0:T(8,128)(2,1)} fusion(bf16[8,4,16,128]{3,2,1,0:T(8,128)(2,1)} %constant_dynamic-update-slice_fusion.2, bf16[4,128,128]{2,1,0:T(8,128)(2,1)S(1)} %convolution_convert_fusion), kind=kLoop, calls=%fused_computation.46 | loop fusion | bytes 32768
  13.7 0.6 %constant_dynamic-update-slice_fusion = bf16[8,4,16,128]{3,2,1,0:T(8,128)(2,1)} fusion(bf16[8,4,16,128]{3,2,1,0:T(8,128)(2,1)} %constant_dynamic-update-slice_fusion.1, bf16[4,128,128]{2,1,0:T(8,128)(2,1)S(1)} %convolution_convert_fusion), kind=kLoop, calls=%fused_computation.45 | loop fusion | bytes 32768 | tf_op jit(solution)/shard_map/stack | solution.py:30
  14.3 0.0 copy-start.3
  14.3 7.3 %all-to-all-start = ((bf16[8,4,16,128]{3,2,1,0:T(8,128)(2,1)}), bf16[8,4,16,128]{3,2,1,0:T(8,128)(2,1)S(1)}, u32[]{:S(2)}, u32[]{:S(2)}) async-start(bf16[8,4,16,128]{3,2,1,0:T(8,128)(2,1)} %constant_dynamic-update-slice_fusion), calls=%async_computation | async-start | bytes 262144 | tf_op jit(solution)/shard_map/all_to_all | solution.py:29
  21.6 0.0 copy-done.3
  21.7 7.3 %all-to-all-done = bf16[8,4,16,128]{3,2,1,0:T(8,128)(2,1)S(1)} async-done(((bf16[8,4,16,128]{3,2,1,0:T(8,128)(2,1)}), bf16[8,4,16,128]{3,2,1,0:T(8,128)(2,1)S(1)}, u32[]{:S(2)}, u32[]{:S(2)}) %all-to-all-start) | async-done | bytes 131104 | tf_op jit(solution)/shard_map/all_to_all | solution.py:29
  29.0 1.5 %add_convert_fusion = bf16[32,16,128]{2,1,0:T(8,128)(2,1)} fusion(bf16[32,16,128]{2,1,0:T(8,128)(2,1)S(1)} %bitcast.202, f32[128]{0:T(128)S(1)} %get-tuple-element.126, f32[128]{0:T(128)S(1)} %get-tuple-element.127, f32[128]{0:T(128)S(1)} %get-tuple-element.88, f32[128]{0:T(128)S(1)} %get-tuple-element.89, f32[128]{0:T(128)S(1)} %get-tuple-element.90, ...), kind=kLoop, calls=%fused_computation.41 | loop fusion | flops 8060928 | bytes 283136 | tf_op jit(solution)/shard_map/convert_element_type | solution.py:47
  (46 shorter events, 1.1 us)
Async XLA Ops:
  0.0 9.2 %copy-start = (bf16[1,128,256]{2,1,0:T(8,128)(2,1)S(1)}, bf16[1,128,256]{2,1,0:T(8,128)(2,1)}, u32[]{:S(2)}) copy-start(bf16[1,128,256]{2,1,0:T(8,128)(2,1)} %param.9) | copy-start | bytes 196612
  3.0 0.7 %copy-start.2 = (f32[41,128]{1,0:T(8,128)S(1)}, f32[41,128]{1,0:T(8,128)}, u32[]{:S(2)}) copy-start(f32[41,128]{1,0:T(8,128)} %param.7) | copy-start | bytes 62980
  3.8 0.9 %copy-start.1 = (bf16[4,128,128]{2,1,0:T(8,128)(2,1)S(1)}, bf16[4,128,128]{2,1,0:T(8,128)(2,1)}, u32[]{:S(2)}) copy-start(bf16[4,128,128]{2,1,0:T(8,128)(2,1)} %param.5) | copy-start | bytes 393220
  14.3 7.3 %copy-start.3 = (f32[41,128]{1,0:T(8,128)S(1)}, f32[41,128]{1,0:T(8,128)}, u32[]{:S(2)}) copy-start(f32[41,128]{1,0:T(8,128)} %param.8) | copy-start | bytes 62980
  14.3 14.7 %all-to-all-start = ((bf16[8,4,16,128]{3,2,1,0:T(8,128)(2,1)}), bf16[8,4,16,128]{3,2,1,0:T(8,128)(2,1)S(1)}, u32[]{:S(2)}, u32[]{:S(2)}) async-start(bf16[8,4,16,128]{3,2,1,0:T(8,128)(2,1)} %constant_dynamic-update-slice_fusion), calls=%async_computation | async-start | bytes 262144 | tf_op jit(solution)/shard_map/all_to_all | solution.py:29
